TPU v7x, 32 devices: a whole 2x2x4 slice. The times are simulated.
32 devices in a mesh: region: 4 (over y, x), tile: 8 (over z, core).
Axes of the slice: x: 2, y: 2, z: 4, core: 2. Of those that a mesh axis runs over, the one named last changes fastest.
Arguments:
- estimate: float32 [32, 128, 512], P('region', 'tile'), may hold values from 0.5 to 18
- observed: float32 [32, 16, 32, 512], P('region', 'tile'), may hold values from 0.3 to 3
- tile_offset: int32 [16], P('tile'), may hold values from 0 to 96
- tile_view: int32 [16], P('tile'), may hold values from 0 to 5
- psf_taps: float32 [6, 3, 3, 15], replicated, may hold values from 0.01 to 0.1
- view_weight: float32 [6], replicated, may hold values from 0.5 to 2
Outputs:
- updated: float32 [32, 128, 512], P('region', 'tile')
All inputs are finite; a program needn't handle non-finite values.
Results may differ from a plain program's by a relative error of at most 0.0003.
Values sent between devices are 32-bit elements; how exact they have to be, the bound alone decides.
No kernel may reach another device: no remote copies, remote signals or barrier semaphores. Data moves between devices by JAX's collectives and lax.ppermute only.
A program may use at most 128 MiB of HBM per device.

v0:
```python
import jax
import jax.numpy as jnp
from jax import lax
from jax.sharding import PartitionSpec as P

PRIOR_WEIGHT = 0.25
MATMUL_PRECISION = lax.Precision.HIGH


def with_halo(cells, sides, width):
    for axis, dim in sides:
        count = lax.axis_size(axis)
        ends = count - 1
        head = lax.slice_in_dim(cells, 0, width, axis=dim)
        tail = lax.slice_in_dim(cells, cells.shape[dim] - width, cells.shape[dim], axis=dim)
        cells = jnp.concatenate(
            [
                lax.ppermute(tail, axis, [(i, (i + 1) % count) for i in range(ends)]),
                cells,
                lax.ppermute(head, axis, [((i + 1) % count, i) for i in range(ends)]),
            ],
            axis=dim,
        )
    return cells


def band(taps, rows, cols, shift):
    kt = taps.shape[-1]
    i = lax.broadcasted_iota(jnp.int32, (rows, cols), 0)
    j = lax.broadcasted_iota(jnp.int32, (rows, cols), 1)
    d = j - i - jnp.asarray(shift, jnp.int32)[..., None, None]
    out = jnp.zeros(d.shape[:-2] + (rows, cols), jnp.float32)
    out = jnp.broadcast_to(out, taps.shape[:-1] + (rows, cols))
    for k in range(kt):
        out = jnp.where(d == k, taps[..., k, None, None], out)
    return out


def kron_band(taps_a, taps_b, rows_a, rows_b, span_b, cols, shift_a, shift_b):
    kt = taps_a.shape[-1]
    lead = taps_a.shape[:-1]
    ia = lax.broadcasted_iota(jnp.int32, (rows_a, cols), 0)
    ca = lax.broadcasted_iota(jnp.int32, (rows_a, cols), 1) // span_b
    ib = lax.broadcasted_iota(jnp.int32, (rows_b, cols), 0)
    cb = lax.broadcasted_iota(jnp.int32, (rows_b, cols), 1) % span_b
    da = ca - ia - jnp.asarray(shift_a, jnp.int32)[..., None, None]
    db = cb - ib - jnp.asarray(shift_b, jnp.int32)[..., None, None]
    ea = jnp.zeros(lead + (rows_a, cols), jnp.float32)
    eb = jnp.zeros(lead + (rows_b, cols), jnp.float32)
    for k in range(kt):
        ea = jnp.where(da == k, taps_a[..., k, None, None], ea)
        eb = jnp.where(db == k, taps_b[..., k, None, None], eb)
    return ea[..., :, None, :] * eb[..., None, :, :]


def depth_band(taps, depth, block):
    kt = taps.shape[-1]
    half = (kt - 1) // 2
    i = lax.broadcasted_iota(jnp.int32, (3 * block, block), 0)
    j = lax.broadcasted_iota(jnp.int32, (3 * block, block), 1)
    d = i - block - j + half
    strip = jnp.zeros(taps.shape[:-1] + (3 * block, block), jnp.float32)
    for k in range(kt):
        strip = jnp.where(d == k, taps[..., k, None, None], strip)
    nb = depth // block
    lead = taps.shape[:-1]
    cols = []
    for b in range(nb):
        col = jnp.pad(strip, [(0, 0)] * len(lead) + [(b * block, (nb - 1 - b) * block), (0, 0)])
        cols.append(col[..., block : block + depth, :])
    return jnp.concatenate(cols, axis=-1)


def on_device(estimate, observed, tile_offset, tile_view, psf_taps, view_weight):
    kt = psf_taps.shape[3]
    rim = (kt - 1) // 2
    block_x, block_y, depth = estimate.shape
    tile_count = observed.shape[1]
    tile_rows = observed.shape[2]
    rank_terms = psf_taps.shape[1]
    group_size = lax.axis_size("tile")
    region_rows = block_y * group_size
    win_rows = -(-(tile_rows + 2 * rim) // 8) * 8
    win_x = block_x + 2 * rim
    tile_info = jnp.stack([tile_offset.astype(jnp.float32), view_weight[tile_view]], axis=1)
    all_info = lax.all_gather(tile_info, "tile", tiled=True)
    all_offset = all_info[:, 0].astype(jnp.int32)
    all_weight = all_info[:, 1]
    core = lax.all_gather(estimate, "tile", axis=1, tiled=True)
    count = lax.axis_size("region")
    lower = lax.ppermute(
        estimate[block_x - rim :], "region", [(i, i + 1) for i in range(count - 1)]
    )
    upper = lax.ppermute(estimate[:rim], "region", [(i + 1, i) for i in range(count - 1)])
    rims = lax.all_gather(jnp.concatenate([lower, upper], axis=0), "tile", axis=1, tiled=True)
    gathered = jnp.concatenate([rims[:rim], core, rims[rim:]], axis=0)
    filters = psf_taps[tile_view]
    weight = view_weight[tile_view]
    ax = filters[:, :, 0]
    ay = filters[:, :, 1]
    az = filters[:, :, 2]
    starts = jnp.clip(tile_offset - rim, 0, region_rows - win_rows)
    shifts = tile_offset - rim - starts
    windows = jnp.stack(
        [lax.dynamic_slice_in_dim(gathered, starts[j], win_rows, 1) for j in range(tile_count)]
    ).reshape(tile_count, win_x * win_rows, depth)
    kxy = kron_band(
        ax, ay, block_x, tile_rows, win_rows, win_x * win_rows, 0, shifts[:, None]
    ).reshape(tile_count, rank_terms * block_x * tile_rows, win_x * win_rows)
    tz = depth_band(az, depth, 128)
    cells = block_x * tile_rows
    part = jnp.einsum("tmk,tkz->tmz", kxy, windows, precision=MATMUL_PRECISION)
    part = part.reshape(tile_count, rank_terms, cells, depth)
    blurred = jnp.einsum("tqmz,tqzn->tmn", part, tz, precision=MATMUL_PRECISION)
    quotient = observed.transpose(1, 0, 2, 3).reshape(tile_count, cells, depth) / blurred
    fxy = kron_band(
        ax[..., ::-1], ay[..., ::-1], block_x, tile_rows, tile_rows, cells, -rim, -rim
    ).reshape(tile_count, rank_terms * cells, cells)
    part = jnp.einsum("tmk,tkz->tmz", fxy, quotient, precision=MATMUL_PRECISION)
    part = part.reshape(tile_count, rank_terms, cells, depth)
    correction = jnp.einsum("tqmz,tqnz->tmn", part, tz, precision=MATMUL_PRECISION)
    weighted = (weight[:, None, None] * correction).reshape(tile_count, block_x, tile_rows, depth)
    numerator = jnp.zeros((block_x, region_rows, depth), jnp.float32)
    for j in range(tile_count):
        current = lax.dynamic_slice_in_dim(numerator, tile_offset[j], tile_rows, 1)
        numerator = lax.dynamic_update_slice_in_dim(
            numerator, current + weighted[j], tile_offset[j], 1
        )
    own_numerator = lax.psum_scatter(numerator, "tile", scatter_dimension=1, tiled=True)
    me = lax.axis_index("tile")
    rows = me * block_y + jnp.arange(block_y, dtype=jnp.int32)
    inside = (rows[None, :] >= all_offset[:, None]) & (
        rows[None, :] < all_offset[:, None] + tile_rows
    )
    own_coverage = jnp.sum(jnp.where(inside, all_weight[:, None], 0.0), axis=0)
    return estimate * (own_numerator + PRIOR_WEIGHT) / (own_coverage[None, :, None] + PRIOR_WEIGHT)


def solution(mesh):
    return jax.shard_map(
        on_device,
        mesh=mesh,
        in_specs=(
            P("region", "tile", None),
            P("region", "tile", None, None),
            P("tile"),
            P("tile"),
            P(),
            P(),
        ),
        out_specs=P("region", "tile", None),
        check_vma=False,
    )
```

profile of v0, /device:TPU:0, one launch (start us, length us, event | category | flops | bytes accessed | tf_op | source)
XLA Modules:
  0.0 163.6 jit_solution(2711943102630633958)
XLA Ops:
  6.5 1.1 fusion.82
  7.7 4.9 %collective-permute-start = (f32[7,16,512]{2,1,0:T(8,128)S(1)}, f32[7,16,512]{2,1,0:T(8,128)S(1)}, u32[]{:S(2)}, u32[]{:S(2)}) collective-permute-start(f32[7,16,512]{2,1,0:T(8,128)S(1)} %get-tuple-element.15), channel_id=1, source_target_pairs={{0,8},{8,16},{16,24},{1,9},{9,17},{17,25},{2,10},{10,18},{18,26},{... | collective-permute-start | bytes 688136 | tf_op jit(solution)/shard_map/ppermute | solution.py:91
  12.5 1.3 collective-permute-start.1
  13.8 3.5 %collective-permute-done = f32[7,16,512]{2,1,0:T(8,128)S(1)} collective-permute-done((f32[7,16,512]{2,1,0:T(8,128)S(1)}, f32[7,16,512]{2,1,0:T(8,128)S(1)}, u32[]{:S(2)}, u32[]{:S(2)}) %collective-permute-start) | collective-permute-done | bytes 229408 | tf_op jit(solution)/shard_map/ppermute | solution.py:91
  17.4 6.9 %collective-permute-done.1 = f32[7,16,512]{2,1,0:T(8,128)S(1)} collective-permute-done((f32[7,16,512]{2,1,0:T(8,128)S(1)}, f32[7,16,512]{2,1,0:T(8,128)S(1)}, u32[]{:S(2)}, u32[]{:S(2)}) %collective-permute-start.1) | collective-permute-done | bytes 229408 | tf_op jit(solution)/shard_map/ppermute | solution.py:94
  24.2 0.8 pad_maximum_fusion.12
  38.3 1.5 select_select_fusion
  39.8 2.9 %pad_slice_fusion.3 = (f32[2,3,512,128]{3,2,1,0:T(8,128)}, f32[2,3,512,128]{3,2,1,0:T(8,128)}, f32[2,3,512,128]{3,2,1,0:T(8,128)}, f32[2,3,512,128]{3,2,1,0:T(8,128)}) fusion(f32[2,3,384,128]{3,2,1,0:T(8,128)S(1)} %select_select_fusion), kind=kLoop, calls=%fused_computation.14 | loop fusion | bytes 7471104 | tf_op jit(solution)/shard_map/slice | solution.py:70
  42.7 1.1 copy.193
  49.0 1.4 select_select_fusion.1
  50.4 3.7 %broadcast_multiply_fusion = f32[2,3,8,32,1056]{4,3,2,1,0:T(8,128)} fusion(f32[2,3,32,1056]{3,2,1,0:T(8,128)S(1)} %select_select_fusion.1, f32[2,3,8,1056]{3,2,1,0:T(8,128)S(1)} %select_select_fusion.2), kind=kLoop, calls=%fused_computation.10 | loop fusion | flops 1622016 | bytes 7501824 | tf_op jit(solution)/shard_map/mul | solution.py:53
  54.1 13.9 %all-gather.4.cloned.1.call-done = f32[14,128,512]{2,1,0:T(8,128)} async-done(((f32[14,16,512]{2,1,0:T(8,128)}), f32[14,128,512]{2,1,0:T(8,128)}) %all-gather.4.cloned.1.call-update) | async-done | bytes 3670032 | tf_op jit(solution)/shard_map/all_gather | solution.py:95
  68.1 3.8 %fusion.80 = (f32[7,128,512]{2,1,0:T(8,128)S(1)}, f32[7,128,512]{2,1,0:T(8,128)}) fusion(f32[14,128,512]{2,1,0:T(8,128)} %all-gather.4.cloned.1.call-done), kind=kLoop, calls=%fused_computation.146 | loop fusion | bytes 7340032 | tf_op jit(solution)/shard_map/slice | solution.py:96
  71.9 25.8 %all-gather.6.cloned.1.call-done = f32[8,128,512]{2,1,0:T(8,128)} async-done(((f32[8,16,512]{2,1,0:T(8,128)}), f32[8,128,512]{2,1,0:T(8,128)}) %all-gather.6.cloned.1.call-update) | async-done | bytes 2097168 | tf_op jit(solution)/shard_map/all_gather | solution.py:89
  97.7 3.0 %pad_maximum_fusion.1 = f32[22,128,512]{2,1,0:T(8,128)S(1)} fusion(f32[7,128,512]{2,1,0:T(8,128)} %get-tuple-element.8, f32[8,128,512]{2,1,0:T(8,128)} %all-gather.6.cloned.1.call-done, f32[7,128,512]{2,1,0:T(8,128)S(1)} %get-tuple-element.7), kind=kLoop, calls=%fused_computation.3 | loop fusion | flops 2883584 | bytes 11534336 | tf_op jit(solution)/shard_map/concatenate | solution.py:96
  100.7 0.8 constant_dynamic-slice_fusion.1
  102.0 6.6 %fusion = f32[2,768,512]{2,1,0:T(8,128)S(1)} fusion(f32[2,768,1056]{2,1,0:T(8,128)S(1)} %bitcast.97, f32[1,1056,512]{2,1,0:T(8,128)S(1)} %bitcast.100, f32[1,1056,512]{2,1,0:T(8,128)S(1)} %bitcast.99), kind=kOutput, calls=%fused_computation.4 | convolution fusion | flops 4983914496 | bytes 13959168 | tf_op jit(solution)/shard_map/tmk,tkz->tmz/dot_general | solution.py:112
  108.7 3.3 %bitcast_divide_fusion = f32[2,256,512]{2,1,0:T(8,128)S(1)} fusion(f32[8,2,32,512]{3,2,0,1:T(8,128)S(1)} %copy-done.9, f32[2,3,256,512]{3,2,1,0:T(8,128)S(1)} %bitcast.102, f32[2,3,512,128]{3,2,1,0:T(8,128)S(1)} %copy-done.4, f32[2,3,512,128]{3,2,1,0:T(8,128)S(1)} %copy-done.5, f32[2,3,512,128]{3,2,1,0:T(8,128)S(1)} %copy-done.6, ...), kind=kOutput, calls=%fused_computation.34 | convolution fusion | flops 2420899840 | bytes 11534336 | tf_op jit(solution)/shard_map/tqmz,tqzn->tmn/dot_general | solution.py:114
  112.0 1.5 fusion.90
  113.5 3.0 %fusion.8 = f32[2,256,512]{2,1,0:T(8,128)S(1)} fusion(f32[2,3,256,512]{3,2,1,0:T(8,128)S(1)} %bitcast.98, f32[2,3,512,128]{3,2,1,0:T(8,128)S(1)} %copy-done.4, f32[2,3,512,128]{3,2,1,0:T(8,128)S(1)} %copy-done.5, f32[2,3,512,128]{3,2,1,0:T(8,128)S(1)} %copy-done.6, f32[2,3,512,128]{3,2,1,0:T(8,128)S(1)} %copy-done.3, f32[2]{0:T(128)S(1)} %gather_fusion), kind=kOutput, calls=%fused_computation.32 | convolution fusion | flops 2420899840 | bytes 10485768 | tf_op jit(solution)/shard_map/tqmz,tqnz->tmn/dot_general | solution.py:121
  118.5 1.3 copy-done.2
  120.0 10.4 %all-gather = f32[8,2,2]{2,1,0:T(2,128)S(1)} all-gather(f32[1,2,2]{2,1,0:T(2,128)S(1)} %bitcast.185), channel_id=1, replica_groups=mesh['region'=4,'tile'=8] {'tile'}, dimensions={0}, use_global_device_ids=true | all-gather | bytes 144 | tf_op jit(solution)/shard_map/all_gather | solution.py:86
  130.8 24.6 %reduce-scatter.2.cloned.1.call-done = f32[8,16,512]{2,1,0:T(8,128)} async-done(((f32[8,128,512]{2,1,0:T(8,128)}), f32[8,16,512]{2,1,0:T(8,128)}) %reduce-scatter.2.cloned.1.call-update) | async-done | bytes 262160 | tf_op jit(solution)/shard_map/reduce_scatter | solution.py:129
  155.3 1.8 %multiply_divide_fusion = f32[8,16,512]{2,1,0:T(8,128)} fusion(f32[8,16,512]{2,1,0:T(8,128)S(1)} %copy-done.7, f32[8,16,512]{2,1,0:T(8,128)} %reduce-scatter.2.cloned.1.call-done, f32[16]{0:T(128)S(1)} %broadcast_add_fusion.2), kind=kLoop, calls=%fused_computation.39 | loop fusion | flops 196608 | bytes 786496 | tf_op jit(solution)/shard_map/div | solution.py:136
  (125 shorter events, 13.5 us)
Async XLA Ops:
  6.5 25.8 %copy-start = (f32[6,3,3,15]{3,2,1,0:T(4,128)S(1)}, f32[6,3,3,15]{3,2,1,0:T(4,128)}, u32[]{:S(2)}) copy-start(f32[6,3,3,15]{3,2,1,0:T(4,128)} %param.10) | copy-start | bytes 9724
  6.5 19.4 %copy-start.10 = (s32[2]{0:T(128)S(1)}, s32[2]{0:T(128)}, u32[]{:S(2)}) copy-start(s32[2]{0:T(128)} %param.8) | copy-start | bytes 28
  6.5 19.4 %copy-start.11 = (s32[2]{0:T(128)S(1)}, s32[2]{0:T(128)}, u32[]{:S(2)}) copy-start(s32[2]{0:T(128)} %param.9) | copy-start | bytes 28
  6.5 61.6 %all-gather.4.cloned.1.call-start = ((), (), s32[]{:S(2)}) async-start(), calls=%async_computation.1 | async-start | bytes 4128768 | tf_op jit(solution)/shard_map/all_gather | solution.py:95
  7.7 9.7 %collective-permute-start = (f32[7,16,512]{2,1,0:T(8,128)S(1)}, f32[7,16,512]{2,1,0:T(8,128)S(1)}, u32[]{:S(2)}, u32[]{:S(2)}) collective-permute-start(f32[7,16,512]{2,1,0:T(8,128)S(1)} %get-tuple-element.15), channel_id=1, source_target_pairs={{0,8},{8,16},{16,24},{1,9},{9,17},{17,25},{2,10},{10,18},{18,26},{... | collective-permute-start | bytes 688136 | tf_op jit(solution)/shard_map/ppermute | solution.py:91
  12.5 11.7 %collective-permute-start.1 = (f32[7,16,512]{2,1,0:T(8,128)S(1)}, f32[7,16,512]{2,1,0:T(8,128)S(1)}, u32[]{:S(2)}, u32[]{:S(2)}) collective-permute-start(f32[7,16,512]{2,1,0:T(8,128)S(1)} %get-tuple-element.16), channel_id=1, source_target_pairs={{8,0},{16,8},{24,16},{9,1},{17,9},{25,17},{10,2},{18,10},{26,18},{... | collective-permute-start | bytes 688136 | tf_op jit(solution)/shard_map/ppermute | solution.py:94
  25.0 72.7 %all-gather.6.cloned.1.call-start = ((), (), s32[]{:S(2)}) async-start(), calls=%async_computation.2 | async-start | bytes 2359296 | tf_op jit(solution)/shard_map/all_gather | solution.py:89
  25.8 129.5 %reduce-scatter.2.cloned.1.call-start = ((), (), s32[]{:S(2)}) async-start(), calls=%async_computation.3 | async-start | bytes 2359296 | tf_op jit(solution)/shard_map/reduce_scatter | solution.py:129
  39.8 2.9 %copy-start.8 = (f32[8,2,32,512]{3,2,1,0:T(8,128)S(1)}, f32[8,2,32,512]{3,2,1,0:T(8,128)}, u32[]{:S(2)}) copy-start(f32[8,2,32,512]{3,2,1,0:T(8,128)} %param.7) | copy-start | bytes 3145732
  42.7 1.1 copy-start.1
  97.7 3.8 %slice-start = ((s8[7077888]{0:T(1024)(128)(4,1)}), s8[4194304]{0:T(1024)(128)(4,1)S(1)}, s32[]{:S(2)}) async-start(s8[7077888]{0:T(1024)(128)(4,1)} %bitcast.95), calls=%async_computation.4 | async-start | bytes 8388608
  97.7 4.3 %slice-start.1 = ((s8[7077888]{0:T(1024)(128)(4,1)}), s8[2883584]{0:T(1024)(128)(4,1)S(1)}, s32[]{:S(2)}) async-start(s8[7077888]{0:T(1024)(128)(4,1)} %bitcast.95), calls=%async_computation.5 | async-start | bytes 5767168
  102.0 6.6 %copy-start.3 = (f32[2,3,512,128]{3,2,1,0:T(8,128)S(1)}, f32[2,3,512,128]{3,2,1,0:T(8,128)}, u32[]{:S(2)}) copy-start(f32[2,3,512,128]{3,2,1,0:T(8,128)} %get-tuple-element.9) | copy-start | bytes 4718596
  102.0 6.7 %copy-start.4 = (f32[2,3,512,128]{3,2,1,0:T(8,128)S(1)}, f32[2,3,512,128]{3,2,1,0:T(8,128)}, u32[]{:S(2)}) copy-start(f32[2,3,512,128]{3,2,1,0:T(8,128)} %get-tuple-element.10) | copy-start | bytes 4718596
  102.0 6.7 %copy-start.5 = (f32[2,3,512,128]{3,2,1,0:T(8,128)S(1)}, f32[2,3,512,128]{3,2,1,0:T(8,128)}, u32[]{:S(2)}) copy-start(f32[2,3,512,128]{3,2,1,0:T(8,128)} %get-tuple-element.11) | copy-start | bytes 4718596
  102.0 6.7 %copy-start.6 = (f32[2,3,512,128]{3,2,1,0:T(8,128)S(1)}, f32[2,3,512,128]{3,2,1,0:T(8,128)}, u32[]{:S(2)}) copy-start(f32[2,3,512,128]{3,2,1,0:T(8,128)} %get-tuple-element.12) | copy-start | bytes 4718596
  102.0 6.7 %copy-start.9 = (f32[8,2,32,512]{3,2,0,1:T(8,128)S(1)}, f32[8,2,32,512]{3,2,0,1:T(8,128)}, u32[]{:S(2)}) copy-start(f32[8,2,32,512]{3,2,0,1:T(8,128)} %copy.193) | copy-start | bytes 3145732
  117.7 37.6 %copy-start.7 = (f32[8,16,512]{2,1,0:T(8,128)S(1)}, f32[8,16,512]{2,1,0:T(8,128)}, u32[]{:S(2)}) copy-start(f32[8,16,512]{2,1,0:T(8,128)} %param.6) | copy-start | bytes 786436
  118.5 1.4 copy-start.2
Sparse Core Ops, SparseCore 0:
  25.2 42.8 all-gather.3
  69.7 27.9 all-gather.5
  120.0 35.2 reduce-scatter.1
where the time goes:
time: 164 us
  waiting for transfers between devices  75.4 us (46%)
  between operations  21.2 us (13%)
  local copies, waits for them, and re-layouts  20.8 us (13%)
  other arithmetic  15 us (9%)
  matrix products  14.4 us (9%)
  blocking collectives  10.4 us (6%)
  starting transfers between devices  6.23 us (4%)
    all_gather x1, waiting for transfers between devices, on_device(): core = lax.all_gather(estimate, 'tile', axis=1, tiled=True)  25.8 us
    reduce_scatter x1, waiting for transfers between devices, on_device(): lax.psum_scatter(numerator, 'tile', scatter_dimension=1, tiled=True)  24.6 us
    all_gather x1, waiting for transfers between devices, on_device(): lax.all_gather(jnp.concatenate([lower, upper], axis=0), 'tile', axis=1, t...  13.9 us
    all_gather x1, blocking collectives, on_device(): all_info = lax.all_gather(tile_info, 'tile', tiled=True)  10.4 us
    ppermute x1, waiting for transfers between devices, on_device(): lax.ppermute(estimate[:rim], 'region', [(i + 1, i) for i in range(count -...  6.86 us
    dot_general x1, matrix products, on_device(): part = jnp.einsum('tmk,tkz->tmz', kxy, windows, precision=MATMUL_PRECISION)  6.62 us
    ppermute x1, starting transfers between devices, on_device(): lax.ppermute(estimate[block_x - rim:], 'region', [(i, i + 1) for i in ran...  4.86 us
    mul x2, other arithmetic, kron_band(): return ea[..., :, None, :] * eb[..., None, :, :]  3.9 us
  transfers between devices with their start and end apart: 5, of which 5 were waited for; matrix products, arithmetic and copies ran while one was open for 15% of the time, Pallas kernels for 0%

commit v1 on v0

--- a/solution.py
+++ b/solution.py
@@ -5,6 +5,33 @@
 
 PRIOR_WEIGHT = 0.25
 MATMUL_PRECISION = lax.Precision.HIGH
+
+
+def shape_the_circles(patch, along_dim):
+    long_array = list(patch.shape[1:])
+    long_array[along_dim] *= patch.shape[0]
+    return jnp.moveaxis(patch, 0, along_dim).reshape(long_array)
+
+
+def obtain_space_by_axis(tile_in, row_axis):
+    n_axis = lax.axis_size(row_axis)
+    current_value = tile_in[None]
+    for at in range(n_axis.bit_length() - 1):
+        b_next = 1 << at
+        shelf = []
+        for idx in tuple(range(n_axis)):
+            shelf.append((idx, idx ^ b_next))
+        v1 = lax.ppermute(current_value, row_axis, shelf)
+        carry_out = jnp.stack([current_value, v1], 0)
+        finding = lax.axis_index(row_axis) >> at & 1
+        current_value = jnp.where(finding == 0, carry_out, carry_out[::-1]).reshape(
+            -1, *tile_in.shape
+        )
+    return current_value
+
+
+def perform_types_for(chunk, view, at_axis):
+    return shape_the_circles(obtain_space_by_axis(chunk, view), at_axis)
 
 
 def with_halo(cells, sides, width):
@@ -92,7 +119,7 @@
         estimate[block_x - rim :], "region", [(i, i + 1) for i in range(count - 1)]
     )
     upper = lax.ppermute(estimate[:rim], "region", [(i + 1, i) for i in range(count - 1)])
-    rims = lax.all_gather(jnp.concatenate([lower, upper], axis=0), "tile", axis=1, tiled=True)
+    rims = perform_types_for(jnp.concatenate([lower, upper], axis=0), "tile", 1)
     gathered = jnp.concatenate([rims[:rim], core, rims[rim:]], axis=0)
     filters = psf_taps[tile_view]
     weight = view_weight[tile_view]

time: 164 us -> 220 us (1.34)
  waiting for transfers between devices: 75.4 us -> 121 us
  starting transfers between devices: 6.23 us -> 11.2 us
  other arithmetic: 15 us -> 18.1 us
    ppermute x0 -> x3, waiting for transfers between devices: none -> 94.2 us  [obtain_space_by_axis(): v1 = lax.ppermute(current_value, row_axis, shelf)]
    all_gather x1, waiting for transfers between devices: 25.8 us -> 0.01 us  [on_device(): core = lax.all_gather(estimate, 'tile', axis=1, tiled=True)]
    all_gather x1 -> x0, waiting for transfers between devices: 13.9 us -> none  [on_device(): lax.all_gather(jnp.concatenate([lower, upper], axis=0), 'tile', axis=1, t...]
    ppermute x1, waiting for transfers between devices: 6.86 us -> 0.01 us  [on_device(): lax.ppermute(estimate[:rim], 'region', [(i + 1, i) for i in range(count -...]
    ppermute x0 -> x3, starting transfers between devices: none -> 4.37 us  [obtain_space_by_axis(): v1 = lax.ppermute(current_value, row_axis, shelf)]
    ppermute x1, waiting for transfers between devices: 3.53 us -> 0.01 us  [on_device(): lax.ppermute(estimate[block_x - rim:], 'region', [(i, i + 1) for i in ran...]
  transfers between devices with their start and end apart: 5 -> 7, of which waited for: 5 -> 3; matrix products, arithmetic and copies ran while one was open for 15% -> 14% of each run, Pallas kernels for 0% -> 0%
where the time goes in v1:
time: 220 us; the launch traced here: 219 us
  waiting for transfers between devices  121 us (55%)
  local copies, waits for them, and re-layouts  21.5 us (10%)
  between operations  21.2 us (10%)
  other arithmetic  18.1 us (8%)
  matrix products  14.5 us (7%)
  blocking collectives  11.9 us (5%)
  starting transfers between devices  11.2 us (5%)
    ppermute x3, waiting for transfers between devices, obtain_space_by_axis(): v1 = lax.ppermute(current_value, row_axis, shelf)  94.2 us
    reduce_scatter x1, waiting for transfers between devices, on_device(): lax.psum_scatter(numerator, 'tile', scatter_dimension=1, tiled=True)  25.9 us
    all_gather x1, blocking collectives, on_device(): all_info = lax.all_gather(tile_info, 'tile', tiled=True)  11.9 us
    dot_general x1, matrix products, on_device(): part = jnp.einsum('tmk,tkz->tmz', kxy, windows, precision=MATMUL_PRECISION)  6.63 us
    ppermute x1, starting transfers between devices, on_device(): lax.ppermute(estimate[block_x - rim:], 'region', [(i, i + 1) for i in ran...  5.55 us
  transfers between devices with their start and end apart: 7, of which 3 were waited for; matrix products, arithmetic and copies ran while one was open for 14% of the time, Pallas kernels for 0%

profile of v1, /device:TPU:0, one launch (start us, length us, event | category | flops | bytes accessed | tf_op | source)
XLA Modules:
  0.0 219.1 jit_solution(18091535045841831435)
XLA Ops:
  7.3 1.1 fusion.84
  8.4 5.5 %collective-permute-start = (f32[7,16,512]{2,1,0:T(8,128)S(1)}, f32[7,16,512]{2,1,0:T(8,128)}, u32[]{:S(2)}, u32[]{:S(2)}) collective-permute-start(f32[7,16,512]{2,1,0:T(8,128)S(1)} %get-tuple-element.18), channel_id=1, source_target_pairs={{0,8},{8,16},{16,24},{1,9},{9,17},{17,25},{2,10},{10,18},{18,26},{... | collective-permute-start | bytes 688136 | tf_op jit(solution)/shard_map/ppermute | solution.py:118
  13.9 1.3 collective-permute-start.1
  15.3 1.3 fusion.90
  23.3 1.5 select_select_fusion
  24.8 2.9 %pad_slice_fusion.3 = (f32[2,3,512,128]{3,2,1,0:T(8,128)}, f32[2,3,512,128]{3,2,1,0:T(8,128)}, f32[2,3,512,128]{3,2,1,0:T(8,128)}, f32[2,3,512,128]{3,2,1,0:T(8,128)}) fusion(f32[2,3,384,128]{3,2,1,0:T(8,128)S(1)} %select_select_fusion), kind=kLoop, calls=%fused_computation.18 | loop fusion | bytes 7471104 | tf_op jit(solution)/shard_map/slice | solution.py:97
  36.1 1.1 copy.196
  40.3 1.1 pad_maximum_fusion.14
  41.5 1.7 collective-permute-start.3
  44.0 20.4 %collective-permute-done.3 = f32[2,14,16,512]{3,2,1,0:T(8,128)S(1)} collective-permute-done((f32[2,14,16,512]{3,2,1,0:T(8,128)S(1)}, f32[2,14,16,512]{3,2,1,0:T(8,128)S(1)}, u32[]{:S(2)}, u32[]{:S(2)}) %collective-permute-start.3) | collective-permute-done | bytes 917536 | tf_op jit(solution)/shard_map/ppermute | solution.py:24
  64.8 2.6 %collective-permute-start.4 = (f32[4,14,16,512]{3,2,1,0:T(8,128)S(1)}, f32[4,14,16,512]{3,2,1,0:T(8,128)S(1)}, u32[]{:S(2)}, u32[]{:S(2)}) collective-permute-start(f32[4,14,16,512]{3,2,1,0:T(8,128)S(1)} %bitcast.119), channel_id=1, source_target_pairs={{0,4},{1,5},{2,6},{3,7},{4,0},{5,1},{6,2},{7,3},{8,12},{9,13},{10,... | collective-permute-start | bytes 5505032 | tf_op jit(solution)/shard_map/ppermute | solution.py:24
  67.8 1.4 select_select_fusion.1
  69.2 3.7 %broadcast_multiply_fusion = f32[2,3,8,32,1056]{4,3,2,1,0:T(8,128)} fusion(f32[2,3,32,1056]{3,2,1,0:T(8,128)S(1)} %select_select_fusion.1, f32[2,3,8,1056]{3,2,1,0:T(8,128)S(1)} %select_select_fusion.2), kind=kLoop, calls=%fused_computation.13 | loop fusion | flops 1622016 | bytes 7501824 | tf_op jit(solution)/shard_map/mul | solution.py:80
  72.9 73.7 %collective-permute-done.4 = f32[4,14,16,512]{3,2,1,0:T(8,128)S(1)} collective-permute-done((f32[4,14,16,512]{3,2,1,0:T(8,128)S(1)}, f32[4,14,16,512]{3,2,1,0:T(8,128)S(1)}, u32[]{:S(2)}, u32[]{:S(2)}) %collective-permute-start.4) | collective-permute-done | bytes 1835040 | tf_op jit(solution)/shard_map/ppermute | solution.py:24
  148.4 1.6 fusion.82
  150.1 3.0 %pad_maximum_fusion.1 = f32[22,128,512]{2,1,0:T(8,128)S(1)} fusion(f32[7,128,512]{2,1,0:T(8,128)} %bitcast.122, f32[8,128,512]{2,1,0:T(8,128)} %all-gather.3.cloned.1.call-done, f32[7,128,512]{2,1,0:T(8,128)S(1)} %bitcast.121), kind=kLoop, calls=%fused_computation.3 | loop fusion | flops 2883584 | bytes 11534336 | tf_op jit(solution)/shard_map/concatenate | solution.py:123
  154.4 6.6 %fusion = f32[2,768,512]{2,1,0:T(8,128)S(1)} fusion(f32[2,768,1056]{2,1,0:T(8,128)S(1)} %bitcast.115, f32[1,1056,512]{2,1,0:T(8,128)S(1)} %bitcast.118, f32[1,1056,512]{2,1,0:T(8,128)S(1)} %bitcast.117), kind=kOutput, calls=%fused_computation.5 | convolution fusion | flops 4983914496 | bytes 13959168 | tf_op jit(solution)/shard_map/tmk,tkz->tmz/dot_general | solution.py:139
  161.1 3.3 %bitcast_divide_fusion = f32[2,256,512]{2,1,0:T(8,128)S(1)} fusion(f32[8,2,32,512]{3,2,0,1:T(8,128)S(1)} %copy-done.10, f32[2,3,256,512]{3,2,1,0:T(8,128)S(1)} %bitcast.124, f32[2,3,512,128]{3,2,1,0:T(8,128)S(1)} %copy-done.5, f32[2,3,512,128]{3,2,1,0:T(8,128)S(1)} %copy-done.6, f32[2,3,512,128]{3,2,1,0:T(8,128)S(1)} %copy-done.7, ...), kind=kOutput, calls=%fused_computation.40 | convolution fusion | flops 2420899840 | bytes 11534336 | tf_op jit(solution)/shard_map/tqmz,tqzn->tmn/dot_general | solution.py:141
  164.4 1.5 fusion.92
  165.9 3.0 %fusion.8 = f32[2,256,512]{2,1,0:T(8,128)S(1)} fusion(f32[2,3,256,512]{3,2,1,0:T(8,128)S(1)} %bitcast.116, f32[2,3,512,128]{3,2,1,0:T(8,128)S(1)} %copy-done.5, f32[2,3,512,128]{3,2,1,0:T(8,128)S(1)} %copy-done.6, f32[2,3,512,128]{3,2,1,0:T(8,128)S(1)} %copy-done.7, f32[2,3,512,128]{3,2,1,0:T(8,128)S(1)} %copy-done.4, f32[2]{0:T(128)S(1)} %gather_fusion), kind=kOutput, calls=%fused_computation.38 | convolution fusion | flops 2420899840 | bytes 10485768 | tf_op jit(solution)/shard_map/tqmz,tqnz->tmn/dot_general | solution.py:148
  170.9 1.3 copy-done.3
  172.4 11.9 %all-gather = f32[8,2,2]{2,1,0:T(2,128)S(1)} all-gather(f32[1,2,2]{2,1,0:T(2,128)S(1)} %bitcast.211), channel_id=1, replica_groups=mesh['region'=4,'tile'=8] {'tile'}, dimensions={0}, use_global_device_ids=true | all-gather | bytes 144 | tf_op jit(solution)/shard_map/all_gather | solution.py:113
  184.6 25.9 %reduce-scatter.2.cloned.1.call-done = f32[8,16,512]{2,1,0:T(8,128)} async-done(((f32[8,128,512]{2,1,0:T(8,128)}), f32[8,16,512]{2,1,0:T(8,128)}) %reduce-scatter.2.cloned.1.call-update) | async-done | bytes 262160 | tf_op jit(solution)/shard_map/reduce_scatter | solution.py:156
  210.5 1.8 multiply_divide_fusion
  (134 shorter events, 18.5 us)
Async XLA Ops:
  6.5 10.8 %copy-start = (f32[6,3,3,15]{3,2,1,0:T(4,128)S(1)}, f32[6,3,3,15]{3,2,1,0:T(4,128)}, u32[]{:S(2)}) copy-start(f32[6,3,3,15]{3,2,1,0:T(4,128)} %param.10) | copy-start | bytes 9724
  6.5 143.6 %all-gather.3.cloned.1.call-start = ((), (), s32[]{:S(2)}) async-start(), calls=%async_computation.1 | async-start | bytes 2359296 | tf_op jit(solution)/shard_map/all_gather | solution.py:116
  7.3 203.3 %reduce-scatter.2.cloned.1.call-start = ((), (), s32[]{:S(2)}) async-start(), calls=%async_computation.2 | async-start | bytes 2359296 | tf_op jit(solution)/shard_map/reduce_scatter | solution.py:156
  8.4 20.8 %collective-permute-start = (f32[7,16,512]{2,1,0:T(8,128)S(1)}, f32[7,16,512]{2,1,0:T(8,128)}, u32[]{:S(2)}, u32[]{:S(2)}) collective-permute-start(f32[7,16,512]{2,1,0:T(8,128)S(1)} %get-tuple-element.18), channel_id=1, source_target_pairs={{0,8},{8,16},{16,24},{1,9},{9,17},{17,25},{2,10},{10,18},{18,26},{... | collective-permute-start | bytes 688136 | tf_op jit(solution)/shard_map/ppermute | solution.py:118
  13.9 16.2 %collective-permute-start.1 = (f32[7,16,512]{2,1,0:T(8,128)S(1)}, f32[7,16,512]{2,1,0:T(8,128)}, u32[]{:S(2)}, u32[]{:S(2)}) collective-permute-start(f32[7,16,512]{2,1,0:T(8,128)S(1)} %get-tuple-element.17), channel_id=1, source_target_pairs={{8,0},{16,8},{24,16},{9,1},{17,9},{25,17},{10,2},{18,10},{26,18},{... | collective-permute-start | bytes 688136 | tf_op jit(solution)/shard_map/ppermute | solution.py:121
  27.7 8.4 %copy-start.9 = (f32[8,2,32,512]{3,2,1,0:T(8,128)S(1)}, f32[8,2,32,512]{3,2,1,0:T(8,128)}, u32[]{:S(2)}) copy-start(f32[8,2,32,512]{3,2,1,0:T(8,128)} %param.7) | copy-start | bytes 3145732
  28.5 8.6 %copy-start.2 = (f32[6]{0:T(128)S(1)}, f32[6]{0:T(128)}, u32[]{:S(2)}) copy-start(f32[6]{0:T(128)} %param.11) | copy-start | bytes 76
  31.1 9.1 %collective-permute-start.2 = (f32[1,14,16,512]{3,2,1,0:T(8,128)S(1)}, f32[1,14,16,512]{3,2,1,0:T(8,128)}, u32[]{:S(2)}, u32[]{:S(2)}) collective-permute-start(f32[1,14,16,512]{3,2,1,0:T(8,128)S(1)} %bitcast.128), channel_id=1, source_target_pairs={{0,1},{1,0},{2,3},{3,2},{4,5},{5,4},{6,7},{7,6},{8,9},{9,8},{10,11... | collective-permute-start | bytes 1376264 | tf_op jit(solution)/shard_map/ppermute | solution.py:24
  41.5 22.8 %collective-permute-start.3 = (f32[2,14,16,512]{3,2,1,0:T(8,128)S(1)}, f32[2,14,16,512]{3,2,1,0:T(8,128)S(1)}, u32[]{:S(2)}, u32[]{:S(2)}) collective-permute-start(f32[2,14,16,512]{3,2,1,0:T(8,128)S(1)} %get-tuple-element.16), channel_id=1, source_target_pairs={{0,2},{1,3},{2,0},{3,1},{4,6},{5,7},{6,4},{7,5},{8,10},{9,11},{10,... | collective-permute-start | bytes 2752520 | tf_op jit(solution)/shard_map/ppermute | solution.py:24
  64.8 81.9 %collective-permute-start.4 = (f32[4,14,16,512]{3,2,1,0:T(8,128)S(1)}, f32[4,14,16,512]{3,2,1,0:T(8,128)S(1)}, u32[]{:S(2)}, u32[]{:S(2)}) collective-permute-start(f32[4,14,16,512]{3,2,1,0:T(8,128)S(1)} %bitcast.119), channel_id=1, source_target_pairs={{0,4},{1,5},{2,6},{3,7},{4,0},{5,1},{6,2},{7,3},{8,12},{9,13},{10,... | collective-permute-start | bytes 5505032 | tf_op jit(solution)/shard_map/ppermute | solution.py:24
  150.1 3.8 %slice-start = ((s8[7077888]{0:T(1024)(128)(4,1)}), s8[4194304]{0:T(1024)(128)(4,1)S(1)}, s32[]{:S(2)}) async-start(s8[7077888]{0:T(1024)(128)(4,1)} %bitcast.113), calls=%async_computation.3 | async-start | bytes 8388608
  150.1 4.3 %slice-start.1 = ((s8[7077888]{0:T(1024)(128)(4,1)}), s8[2883584]{0:T(1024)(128)(4,1)S(1)}, s32[]{:S(2)}) async-start(s8[7077888]{0:T(1024)(128)(4,1)} %bitcast.113), calls=%async_computation.4 | async-start | bytes 5767168
  154.4 6.7 %copy-start.4 = (f32[2,3,512,128]{3,2,1,0:T(8,128)S(1)}, f32[2,3,512,128]{3,2,1,0:T(8,128)}, u32[]{:S(2)}) copy-start(f32[2,3,512,128]{3,2,1,0:T(8,128)} %get-tuple-element.9) | copy-start | bytes 4718596
  154.4 6.7 %copy-start.5 = (f32[2,3,512,128]{3,2,1,0:T(8,128)S(1)}, f32[2,3,512,128]{3,2,1,0:T(8,128)}, u32[]{:S(2)}) copy-start(f32[2,3,512,128]{3,2,1,0:T(8,128)} %get-tuple-element.10) | copy-start | bytes 4718596
  154.4 6.7 %copy-start.6 = (f32[2,3,512,128]{3,2,1,0:T(8,128)S(1)}, f32[2,3,512,128]{3,2,1,0:T(8,128)}, u32[]{:S(2)}) copy-start(f32[2,3,512,128]{3,2,1,0:T(8,128)} %get-tuple-element.11) | copy-start | bytes 4718596
  154.4 6.7 %copy-start.7 = (f32[2,3,512,128]{3,2,1,0:T(8,128)S(1)}, f32[2,3,512,128]{3,2,1,0:T(8,128)}, u32[]{:S(2)}) copy-start(f32[2,3,512,128]{3,2,1,0:T(8,128)} %get-tuple-element.12) | copy-start | bytes 4718596
  154.4 6.7 %copy-start.10 = (f32[8,2,32,512]{3,2,0,1:T(8,128)S(1)}, f32[8,2,32,512]{3,2,0,1:T(8,128)}, u32[]{:S(2)}) copy-start(f32[8,2,32,512]{3,2,0,1:T(8,128)} %copy.196) | copy-start | bytes 3145732
  170.0 42.3 %copy-start.1 = (f32[6,3,3,15]{3,2,1,0:T(4,128)S(1)}, f32[6,3,3,15]{3,2,1,0:T(4,128)}, u32[]{:S(2)}) copy-start(f32[6,3,3,15]{3,2,1,0:T(4,128)} %param.10) | copy-start | bytes 9724
  170.1 40.4 %copy-start.8 = (f32[8,16,512]{2,1,0:T(8,128)S(1)}, f32[8,16,512]{2,1,0:T(8,128)}, u32[]{:S(2)}) copy-start(f32[8,16,512]{2,1,0:T(8,128)} %param.6) | copy-start | bytes 786436
  170.9 1.4 copy-start.3
Sparse Core Ops, SparseCore 0:
  9.0 31.9 all-gather.2
  172.4 38.0 reduce-scatter.1
